TPU v7x, 512 devices: a whole 4x4x16 slice. The times are simulated.
512 devices in a mesh: req: 128 (over z, x, core), tp: 4 (over y).
Axes of the slice: x: 4, y: 4, z: 16, core: 2. Of those that a mesh axis runs over, the one named last changes fastest.
Arguments:
- queries: bfloat16 [16384, 3584], P('req', 'tp'), may hold values from -13 to 13
- tree_kv: bfloat16 [16384, 4, 256], P('req', 'tp'), may hold values from -5 to 5
- page_pool: bfloat16 [1536, 4, 128, 256], P('req', 'tp'), may hold values from -5 to 5
- page_table: int32 [256, 8], P('req'), may hold values from 0 to 11, as said below
- cache_len: int32 [256], P('req'), may hold values from 1 to 1024
- parents: int32 [256, 64], P('req'), may hold values from -1 to 62, as said below
- accepted: int32 [256], P('req'), may hold values from 0 to 63
- o_weight: bfloat16 [3584, 1792], P('tp'), may hold values from -0.5 to 0.5
Outputs:
- projected: bfloat16 [16384, 1792], P(('req', 'tp'))
- kept_rows: bfloat16 [16384, 4, 256], P('req', 'tp')
Inputs may be any that keep to these rules, and one draw needn't show every extreme that they name: Logical page k of request r is in slot page_table[r, k] of its own device's pool for k < 2, among that pool's first 4 slots, and for k >= 2 in that slot of the next req device's pool (the first device after the last), among its last 8 slots; distinct pages are in distinct slots; entries at k >= ceil(cache_len[r] / 128) are 0. parents[r, 0] = -1 and 0 <= parents[r, j] < j for j >= 1.
All inputs are finite; a program needn't handle non-finite values.
Results may differ from a plain program's by a relative error of at most 0.007.
Values may be sent and summed in bfloat16 or wider, within the bound.
No kernel may reach another device: no remote copies, remote signals or barrier semaphores. Data moves between devices by JAX's collectives and lax.ppermute only.
A program may use at most 64 MiB of HBM per device.

v0:
```python
import math
import jax
import jax.numpy as jnp
from jax import lax
from jax.sharding import PartitionSpec as P

HEAD_SIZE = 128
LOCAL = 2
very_negative = -1e30


def from_behind(block, axis, distance):
    devices = range(lax.axis_size(axis))
    route = [((i - distance) % len(devices), i) for i in devices]
    return lax.ppermute(block, axis, route)


def ancestors(parent_row):
    tree_len = parent_row.shape[0]
    node_ids = jnp.arange(tree_len, dtype=jnp.int32)
    parent_links = (parent_row[:, None] == node_ids[None, :]).astype(jnp.float32)
    reachable = jnp.eye(tree_len, dtype=jnp.float32) + parent_links
    for squaring in range((tree_len - 1).bit_length()):
        reachable = jnp.minimum(jnp.dot(reachable, reachable, precision=lax.Precision.HIGHEST), 1.0)
    return reachable


def block_stats(query_rows, block_keys, block_values, visible):
    scores = jnp.einsum(
        "tgd,nd->tgn", query_rows, block_keys, preferred_element_type=jnp.float32
    ) * (1.0 / math.sqrt(query_rows.shape[-1]))
    scores = jnp.where(visible, scores, very_negative)
    maxima = jnp.max(scores, axis=-1)
    weights = jnp.where(visible, jnp.exp(scores - maxima[..., None]), 0.0).astype(jnp.bfloat16)
    totals = jnp.sum(weights.astype(jnp.float32), axis=-1)
    accums = jnp.einsum("tgn,nd->tgd", weights, block_values, preferred_element_type=jnp.float32)
    return (maxima, totals, accums)


def combine(first_state, second_state):
    joined_max = jnp.maximum(first_state[0], second_state[0])
    first_factor = jnp.exp(first_state[0] - joined_max)
    second_factor = jnp.exp(second_state[0] - joined_max)
    totals = first_factor * first_state[1] + second_factor * second_state[1]
    accums = first_factor[..., None] * first_state[2] + second_factor[..., None] * second_state[2]
    return (joined_max, totals, accums)


def pages_partial(query_rows, pages, visible):
    head_dim = query_rows.shape[-1]
    scores = jnp.einsum(
        "tgd,knd->tgkn", query_rows, pages[..., :head_dim], preferred_element_type=jnp.float32
    ) * (1.0 / math.sqrt(head_dim))
    mask = visible[None, None, :, :]
    scores = jnp.where(mask, scores, very_negative)
    maxima = jnp.max(scores, axis=-1)
    weights = jnp.where(mask, jnp.exp(scores - maxima[..., None]), 0.0).astype(jnp.bfloat16)
    totals = jnp.sum(weights.astype(jnp.float32), axis=-1)
    accums = jnp.einsum(
        "tgkn,knd->tgkd", weights, pages[..., head_dim:], preferred_element_type=jnp.float32
    )
    overall = jnp.max(maxima, axis=-1)
    factors = jnp.exp(maxima - overall[..., None])
    total = jnp.sum(factors * totals, axis=-1)
    accum = jnp.sum(factors[..., None] * accums, axis=2)
    return (overall, total, accum)


def sweep_all(query_rows, pool_slots, tables, lengths, first_page):
    page_len = pool_slots.shape[1]
    page_count = tables.shape[1]
    offsets = jnp.arange(page_len, dtype=jnp.int32)
    page_numbers = first_page + jnp.arange(page_count, dtype=jnp.int32)
    positions = page_numbers[:, None] * page_len + offsets[None, :]

    def one_request(request_data):
        request_query, table_row, length = request_data
        pages = jnp.take(pool_slots, table_row, axis=0)
        visible = positions < length
        return pages_partial(request_query, pages, visible)

    return lax.map(one_request, (query_rows, tables, lengths))


def shards(queries, tree_kv, page_pool, page_table, cache_len, parents, accepted, o_weight):
    requests = page_table.shape[0]
    tree_len = parents.shape[1]
    group_size = queries.shape[1] // HEAD_SIZE
    query_rows = queries.reshape(requests, tree_len, group_size, HEAD_SIZE)
    tree_rows = tree_kv[:, 0, :].reshape(requests, tree_len, 2 * HEAD_SIZE)
    pool_slots = page_pool[:, 0]
    reachable = jax.vmap(ancestors)(parents)
    page_meta = jnp.concatenate([page_table, cache_len[:, None]], axis=1)
    moved_queries, moved_meta = from_behind((queries, page_meta), "req", 1)
    moved_rows = moved_queries.reshape(requests, tree_len, group_size, HEAD_SIZE)
    partial_value = sweep_all(
        moved_rows, pool_slots, moved_meta[:, LOCAL:-1], moved_meta[:, -1], LOCAL
    )
    returned = from_behind((partial_value[2], partial_value[0], partial_value[1]), "req", -1)
    local_state = sweep_all(query_rows, pool_slots, page_table[:, :LOCAL], cache_len, 0)
    page_state = combine(local_state, (returned[1], returned[2], returned[0]))
    tree_visible = (reachable > 0.5)[:, :, None, :]
    tree_state = jax.vmap(block_stats)(
        query_rows, tree_rows[:, :, :HEAD_SIZE], tree_rows[:, :, HEAD_SIZE:], tree_visible
    )
    merged = combine(page_state, tree_state)
    attention = (
        (merged[2] / merged[1][..., None])
        .astype(jnp.bfloat16)
        .reshape(requests * tree_len, group_size * HEAD_SIZE)
    )
    rows_out = attention.shape[0] // lax.axis_size("tp")
    whole_sum = lax.psum(jnp.dot(attention, o_weight, preferred_element_type=jnp.float32), "tp")
    summed = lax.dynamic_slice_in_dim(whole_sum, lax.axis_index("tp") * rows_out, rows_out, 0)
    projected = summed.astype(jnp.bfloat16)
    node_ids = jnp.arange(tree_len, dtype=jnp.int32)
    leaf_onehot = (accepted[:, None] == node_ids[None, :]).astype(jnp.float32)
    kept_mask = jnp.einsum("rm,rmn->rn", leaf_onehot, reachable, precision=lax.Precision.HIGHEST)
    depths = jnp.sum(reachable, axis=2) - 1.0
    slot_ids = jnp.arange(tree_len, dtype=jnp.float32)
    selector = (
        kept_mask[:, None, :] * (depths[:, None, :] == slot_ids[None, :, None]).astype(jnp.float32)
    ).astype(jnp.bfloat16)
    kept = jnp.einsum(
        "rsm,rmc->rsc", selector, tree_rows, preferred_element_type=jnp.float32
    ).astype(jnp.bfloat16)
    return (projected, kept.reshape(requests * tree_len, 1, 2 * HEAD_SIZE))


def solution(mesh):
    in_specs = (
        P("req", "tp"),
        P("req", "tp", None),
        P("req", "tp", None, None),
        P("req", None),
        P("req"),
        P("req", None),
        P("req"),
        P("tp", None),
    )
    out_specs = (P(("req", "tp"), None), P("req", "tp", None))
    return jax.shard_map(shards, mesh=mesh, in_specs=in_specs, out_specs=out_specs, check_vma=False)
```

profile of v0, /device:TPU:8, one launch (start us, length us, event | category | flops | bytes accessed | tf_op | source)
XLA Modules:
  0.0 122.9 jit_solution(13484984771491410831)
XLA Ops:
  0.6 0.9 copy.48
  1.5 1.4 %pad_add_fusion = s32[2,9]{1,0:T(2,128)} fusion(s32[2,1]{1,0:T(2,128)S(1)} %copy.48, s32[2,8]{1,0:T(2,128)} %param.15), kind=kLoop, calls=%fused_computation.98 | loop fusion | flops 18 | bytes 144 | tf_op jit(solution)/shard_map/concatenate | solution.py:93
  2.9 1.9 %collective-permute-start = (s32[2,9]{1,0:T(2,128)}, s32[2,9]{1,0:T(2,128)}, u32[]{:S(2)}, u32[]{:S(2)}) collective-permute-start(s32[2,9]{1,0:T(2,128)} %pad_add_fusion), channel_id=1, source_target_pairs={{508,0},{0,4},{4,8},{8,12},{12,16},{16,20},{20,24},{24,28},{28,32}... | collective-permute-start | bytes 224 | tf_op jit(solution)/shard_map/ppermute | solution.py:15
  4.8 3.5 %collective-permute-start.1 = (bf16[128,896]{1,0:T(8,128)(2,1)}, bf16[128,896]{1,0:T(8,128)(2,1)}, u32[]{:S(2)}, u32[]{:S(2)}) collective-permute-start(bf16[128,896]{1,0:T(8,128)(2,1)} %param.12), channel_id=1, source_target_pairs={{508,0},{0,4},{4,8},{8,12},{12,16},{16,20},{20,24},{24,28},{28,32}... | collective-permute-start | bytes 688136 | tf_op jit(solution)/shard_map/ppermute | solution.py:15
  8.9 1.2 reshape.134
  10.1 1.3 %compare_bitcast_fusion = pred[2,64,1]{1,0,2:T(4,128)(4,1)} fusion(s32[2]{0:T(128)} %param.18), kind=kLoop, calls=%fused_computation.97 | loop fusion | flops 128 | bytes 136 | tf_op jit(solution)/shard_map/eq | solution.py:117
  11.4 1.0 convolution_minimum_fusion.5
  13.3 0.8 broadcast_compare_fusion
  14.1 0.8 copy.52
  15.6 1.4 %fusion.35 = f32[2,1,64]{2,1,0:T(1,128)} fusion(f32[2,64,64]{2,1,0:T(8,128)S(1)} %get-tuple-element.262, pred[2,64,1]{1,0,2:T(4,128)(4,1)} %compare_bitcast_fusion), kind=kOutput, calls=%fused_computation.95 | convolution fusion | flops 98304 | bytes 33408 | tf_op jit(solution)/shard_map/rm,rmn->rn/dot_general | solution.py:118
  17.7 0.8 broadcast.143.clone.1
  18.5 17.2 %while.30 = (s32[]{:T(128)}, f32[2,64,7]{1,2,0:T(8,128)S(1)}, f32[2,64,7]{1,2,0:T(8,128)S(1)}, f32[2,64,7,128]{3,1,2,0:T(8,128)}, s32[2]{0:T(128)}, /*index=5*/b...) while((s32[]{:T(128)}, f32[2,64,7]{1,2,0:T(8,128)S(1)}, ...), condition=%wide.region_6.7_spmd.clone, body=%wide.region_0.6_spmd.clone.sunk | while | flops 59991572 | bytes 6568445 | solution.py:82
  18.5 1.3 %dynamic_slice.66 = s32[1]{0:T(128)} dynamic-slice(s32[2]{0:T(128)} %get-tuple-element.465, s32[]{:T(128)S(6)} %copy.108), dynamic_slice_sizes={1} | dynamic-slice | bytes 12 | tf_op jit(solution)/shard_map/while/body/jit(dynamic_index_in_dim)/dynamic_slice | solution.py:82
  19.8 1.3 %add_compare_fusion.4 = pred[2,128]{1,0:T(4,128)(4,1)S(1)} fusion(s32[2]{0:T(128)} %get-tuple-element.469, s32[]{:T(128)} %bitcast.143), kind=kLoop, calls=%fused_computation.28.clone.1 | loop fusion | flops 512 | bytes 268 | tf_op jit(solution)/shard_map/while/body/eval_jaxpr/lt | solution.py:79
  22.5 1.7 %gather_fusion = bf16[2,128,256]{2,1,0:T(8,128)(2,1)S(1)} fusion(bf16[12,128,256]{2,1,0:T(8,128)(2,1)} %get-tuple-element.468, s32[1024]{0:T(1024)S(1)} %pad_clamp_fusion.4), kind=kCustom, calls=%fused_computation.clone.clone.1 | custom fusion | bytes 262152 | tf_op jit(solution)/shard_map/while/body/eval_jaxpr/jit(_take)/gather | solution.py:78
  24.3 1.4 %fusion.68 = (f32[64,7,2]{0,2,1:T(2,128)S(1)}, f32[64,7]{0,1:T(8,128)S(1)}, f32[64,7,2,128]{3,0,2,1:T(8,128)S(1)}) fusion(bf16[2,128,256]{2,1,0:T(8,128)(2,1)S(1)} %broadcast_select_fusion.4, bf16[2,64,7,128]{3,1,2,0:T(8,128)(2,1)} %get-tuple-element.466, s32[]{:T(128)S(6)} %copy.108, pred[2,128]{1,0:T(4,128)(4,1)S(1)} %add_compare_fusion.4), kind=kOutput, calls=%fused_computation.105.clone.1 | convolution fusion | flops 29817536 | bytes 644868 | tf_op jit(solution)/shard_map/while/body/eval_jaxpr/tgd,knd->tgkn/dot_general | solution.py:51
  27.1 1.2 %dynamic_slice.66 = s32[1]{0:T(128)} dynamic-slice(s32[2]{0:T(128)} %get-tuple-element.465, s32[]{:T(128)S(6)} %copy.108), dynamic_slice_sizes={1} | dynamic-slice | bytes 12 | tf_op jit(solution)/shard_map/while/body/jit(dynamic_index_in_dim)/dynamic_slice | solution.py:82
  28.4 1.3 %add_compare_fusion.4 = pred[2,128]{1,0:T(4,128)(4,1)S(1)} fusion(s32[2]{0:T(128)} %get-tuple-element.469, s32[]{:T(128)} %bitcast.143), kind=kLoop, calls=%fused_computation.28.clone.1 | loop fusion | flops 512 | bytes 268 | tf_op jit(solution)/shard_map/while/body/eval_jaxpr/lt | solution.py:79
  31.1 1.7 %gather_fusion = bf16[2,128,256]{2,1,0:T(8,128)(2,1)S(1)} fusion(bf16[12,128,256]{2,1,0:T(8,128)(2,1)} %get-tuple-element.468, s32[1024]{0:T(1024)S(1)} %pad_clamp_fusion.4), kind=kCustom, calls=%fused_computation.clone.clone.1 | custom fusion | bytes 262152 | tf_op jit(solution)/shard_map/while/body/eval_jaxpr/jit(_take)/gather | solution.py:78
  32.9 1.4 %fusion.68 = (f32[64,7,2]{0,2,1:T(2,128)S(1)}, f32[64,7]{0,1:T(8,128)S(1)}, f32[64,7,2,128]{3,0,2,1:T(8,128)S(1)}) fusion(bf16[2,128,256]{2,1,0:T(8,128)(2,1)S(1)} %broadcast_select_fusion.4, bf16[2,64,7,128]{3,1,2,0:T(8,128)(2,1)} %get-tuple-element.466, s32[]{:T(128)S(6)} %copy.108, pred[2,128]{1,0:T(4,128)(4,1)S(1)} %add_compare_fusion.4), kind=kOutput, calls=%fused_computation.105.clone.1 | convolution fusion | flops 29817536 | bytes 644868 | tf_op jit(solution)/shard_map/while/body/eval_jaxpr/tgd,knd->tgkn/dot_general | solution.py:51
  35.7 1.3 %fusion.43 = (f32[2,64,7]{1,2,0:T(8,128)S(1)}, f32[2,64,7,64]{1,3,2,0:T(8,128)S(1)}) fusion(bf16[2,64,7,128]{3,1,2,0:T(8,128)(2,1)} %get-tuple-element.472, bf16[2,64,256]{2,1,0:T(8,128)(2,1)S(1)} %bitcast.156, pred[2,64,64]{1,2,0:T(8,128)(4,1)S(1)} %copy.52), kind=kOutput, calls=%fused_computation.107 | convolution fusion | flops 14851200 | bytes 511488 | tf_op jit(solution)/shard_map/vmap(tgd,nd->tgn)/dot_general | solution.py:29
  37.8 1.0 fusion.26
  40.0 1.3 %slice.29 = s32[2,6]{1,0:T(2,128)} slice(s32[2,9]{1,0:T(2,128)} %collective-permute-done), slice={[0:2], [2:8]} | slice | bytes 96 | tf_op jit(solution)/shard_map/slice | solution.py:97
  41.3 1.4 %slice_reduce_fusion = s32[2]{0:T(128)} fusion(s32[2,9]{1,0:T(2,128)} %collective-permute-done), kind=kLoop, calls=%fused_computation.99 | loop fusion | bytes 16 | tf_op jit(solution)/shard_map/slice | solution.py:97
  42.7 1.2 reshape.135
  45.8 0.8 broadcast.143.clone
  46.7 23.4 %while.31 = (s32[]{:T(128)}, f32[2,64,7]{1,2,0:T(8,128)}, f32[2,64,7]{1,2,0:T(8,128)}, f32[2,64,7,128]{3,1,2,0:T(8,128)}, s32[2]{0:T(128)}, /*index=5*/bf16[2,64...) while((s32[]{:T(128)}, f32[2,64,7]{1,2,0:T(8,128)}, ...), condition=%wide.region_13.14_spmd.clone, body=%wide.region_7.13_spmd.clone.sunk | while | flops 180089152 | bytes 11682033 | solution.py:82
  46.7 1.3 %dynamic_slice.70 = s32[1]{0:T(128)} dynamic-slice(s32[2]{0:T(128)} %get-tuple-element.435, s32[]{:T(128)S(6)} %copy.96), dynamic_slice_sizes={1} | dynamic-slice | bytes 12 | tf_op jit(solution)/shard_map/while/body/jit(dynamic_index_in_dim)/dynamic_slice | solution.py:82
  48.0 1.4 %add_compare_fusion.5 = pred[6,128]{1,0:T(8,128)(4,1)S(1)} fusion(s32[6]{0:T(128)} %get-tuple-element.439, s32[]{:T(128)} %bitcast.153), kind=kLoop, calls=%fused_computation.49.clone.1 | loop fusion | flops 1536 | bytes 796 | tf_op jit(solution)/shard_map/while/body/eval_jaxpr/lt | solution.py:79
  50.1 1.3 %compare_and_fusion.5 = pred[6]{0:T(512)(128)(4,1)} fusion(s32[2,6]{1,0:T(2,128)} %get-tuple-element.437, s32[]{:T(128)S(6)} %copy.96), kind=kLoop, calls=%fused_computation.52.clone.1 | loop fusion | flops 36 | bytes 34 | tf_op jit(solution)/shard_map/while/body/eval_jaxpr/jit(_take)/and | solution.py:78
  51.4 2.5 %gather_fusion.1 = bf16[6,128,256]{2,1,0:T(8,128)(2,1)} fusion(bf16[12,128,256]{2,1,0:T(8,128)(2,1)} %get-tuple-element.438, s32[1024]{0:T(1024)S(1)} %pad_clamp_fusion.5), kind=kCustom, calls=%fused_computation.1.clone.clone.1 | custom fusion | bytes 786456 | tf_op jit(solution)/shard_map/while/body/eval_jaxpr/jit(_take)/gather | solution.py:78
  53.9 1.1 broadcast_select_fusion.5
  55.7 0.8 convert_reduce_fusion.6
  58.4 1.3 %dynamic_slice.70 = s32[1]{0:T(128)} dynamic-slice(s32[2]{0:T(128)} %get-tuple-element.435, s32[]{:T(128)S(6)} %copy.96), dynamic_slice_sizes={1} | dynamic-slice | bytes 12 | tf_op jit(solution)/shard_map/while/body/jit(dynamic_index_in_dim)/dynamic_slice | solution.py:82
  59.7 1.4 %add_compare_fusion.5 = pred[6,128]{1,0:T(8,128)(4,1)S(1)} fusion(s32[6]{0:T(128)} %get-tuple-element.439, s32[]{:T(128)} %bitcast.153), kind=kLoop, calls=%fused_computation.49.clone.1 | loop fusion | flops 1536 | bytes 796 | tf_op jit(solution)/shard_map/while/body/eval_jaxpr/lt | solution.py:79
  61.8 1.3 %compare_and_fusion.5 = pred[6]{0:T(512)(128)(4,1)} fusion(s32[2,6]{1,0:T(2,128)} %get-tuple-element.437, s32[]{:T(128)S(6)} %copy.96), kind=kLoop, calls=%fused_computation.52.clone.1 | loop fusion | flops 36 | bytes 34 | tf_op jit(solution)/shard_map/while/body/eval_jaxpr/jit(_take)/and | solution.py:78
  63.1 2.5 %gather_fusion.1 = bf16[6,128,256]{2,1,0:T(8,128)(2,1)} fusion(bf16[12,128,256]{2,1,0:T(8,128)(2,1)} %get-tuple-element.438, s32[1024]{0:T(1024)S(1)} %pad_clamp_fusion.5), kind=kCustom, calls=%fused_computation.1.clone.clone.1 | custom fusion | bytes 786456 | tf_op jit(solution)/shard_map/while/body/eval_jaxpr/jit(_take)/gather | solution.py:78
  65.5 1.1 broadcast_select_fusion.5
  67.4 0.8 convert_reduce_fusion.6
  70.0 11.4 %collective-permute-start.3 = (f32[2,64,7,128]{3,1,2,0:T(8,128)}, f32[2,64,7,128]{3,1,2,0:T(8,128)}, u32[]{:S(2)}, u32[]{:S(2)}) collective-permute-start(f32[2,64,7,128]{3,1,2,0:T(8,128)} %get-tuple-element.103), channel_id=1, source_target_pairs={{4,0},{8,4},{12,8},{16,12},{20,16},{24,20},{28,24},{32,28},{36,32}... | collective-permute-start | bytes 1376264 | tf_op jit(solution)/shard_map/ppermute | solution.py:15
  81.5 1.4 %convolution_convert_fusion = bf16[2,64,256]{2,1,0:T(8,128)(2,1)} fusion(bf16[2,64,256]{2,1,0:T(8,128)(2,1)S(1)} %bitcast.158, f32[2,64]{1,0:T(2,128)} %bitcast.160, f32[2,64]{1,0:T(2,128)} %broadcast_add_fusion), kind=kOutput, calls=%fused_computation.58 | convolution fusion | flops 4243456 | bytes 132096 | tf_op jit(solution)/shard_map/rsm,rmc->rsc/dot_general | solution.py:124
  82.9 2.6 %collective-permute-start.2 = (f32[2,64,7]{1,2,0:T(8,128)}, f32[2,64,7]{1,2,0:T(8,128)S(1)}, u32[]{:S(2)}, u32[]{:S(2)}) collective-permute-start(f32[2,64,7]{1,2,0:T(8,128)} %get-tuple-element.101), channel_id=1, source_target_pairs={{4,0},{8,4},{12,8},{16,12},{20,16},{24,20},{28,24},{32,28},{36,32}... | collective-permute-start | bytes 10760 | tf_op jit(solution)/shard_map/ppermute | solution.py:15
  85.5 3.7 %collective-permute-start.4 = (f32[2,64,7]{1,2,0:T(8,128)}, f32[2,64,7]{1,2,0:T(8,128)S(1)}, u32[]{:S(2)}, u32[]{:S(2)}) collective-permute-start(f32[2,64,7]{1,2,0:T(8,128)} %get-tuple-element.105), channel_id=1, source_target_pairs={{4,0},{8,4},{12,8},{16,12},{20,16},{24,20},{28,24},{32,28},{36,32}... | collective-permute-start | bytes 10760 | tf_op jit(solution)/shard_map/ppermute | solution.py:15
  89.2 1.1 convert_reduce_fusion.2
  90.8 1.9 %divide_convert_fusion = bf16[2,64,7,128]{3,1,2,0:T(8,128)(2,1)S(1)} fusion(f32[2,64,7,128]{3,1,2,0:T(8,128)} %fusion.26, f32[2,64,7,128]{3,1,2,0:T(8,128)} %collective-permute-done.3, f32[2,64,7,128]{3,1,2,0:T(8,128)} %get-tuple-element.102, f32[2,64,7]{1,2,0:T(8,128)S(1)} %get-tuple-element.250, f32[2,64,7]{1,2,0:T(8,128)S(1)} %get-tuple-element.254, ...), kind=kLoop, calls=%fused_computation.65 | loop fusion | flops 917504 | bytes 1623552 | tf_op jit(solution)/shard_map/convert_element_type | solution.py:109
  92.9 1.6 %fusion.21 = f32[128,1792]{1,0:T(8,128)} fusion(bf16[896,1792]{1,0:T(8,128)(2,1)S(1)} %copy-done, bf16[16,8,7,128]{3,2,1,0:T(8,128)(2,1)S(1)} %bitcast.155), kind=kOutput, calls=%fused_computation.68 | convolution fusion | flops 411041792 | bytes 4358144 | tf_op jit(solution)/shard_map/dot_general | solution.py:113
  94.5 26.9 %all-reduce.1 = bf16[128,1792]{1,0:T(8,128)(2,1)} all-reduce(f32[128,1792]{1,0:T(8,128)} %fusion.21), channel_id=1, replica_groups=mesh['req'=128,'tp'=4] {'tp'}, use_global_device_ids=true, to_apply=%region_16.17 | all-reduce | flops 229376 | bytes 1376256 | tf_op jit(solution)/shard_map/psum | solution.py:113
  121.4 1.6 %dynamic-slice_convert_fusion = bf16[32,1792]{1,0:T(8,128)(2,1)} fusion(bf16[128,1792]{1,0:T(8,128)(2,1)} %all-reduce.1, s32[]{:T(128)S(6)} %select_n.66), kind=kLoop, calls=%fused_computation.71 | loop fusion | bytes 229380 | tf_op jit(solution)/shard_map/convert_element_type | solution.py:115
  (114 shorter events, 19.2 us)
Async XLA Ops:
  0.6 92.2 %copy-start = (bf16[896,1792]{1,0:T(8,128)(2,1)S(1)}, bf16[896,1792]{1,0:T(8,128)(2,1)}, u32[]{:S(2)}) copy-start(bf16[896,1792]{1,0:T(8,128)(2,1)} %param.19) | copy-start | bytes 9633796
  2.9 37.1 %collective-permute-start = (s32[2,9]{1,0:T(2,128)}, s32[2,9]{1,0:T(2,128)}, u32[]{:S(2)}, u32[]{:S(2)}) collective-permute-start(s32[2,9]{1,0:T(2,128)} %pad_add_fusion), channel_id=1, source_target_pairs={{508,0},{0,4},{4,8},{8,12},{12,16},{16,20},{20,24},{24,28},{28,32}... | collective-permute-start | bytes 224 | tf_op jit(solution)/shard_map/ppermute | solution.py:15
  4.8 37.8 %collective-permute-start.1 = (bf16[128,896]{1,0:T(8,128)(2,1)}, bf16[128,896]{1,0:T(8,128)(2,1)}, u32[]{:S(2)}, u32[]{:S(2)}) collective-permute-start(bf16[128,896]{1,0:T(8,128)(2,1)} %param.12), channel_id=1, source_target_pairs={{508,0},{0,4},{4,8},{8,12},{12,16},{16,20},{20,24},{24,28},{28,32}... | collective-permute-start | bytes 688136 | tf_op jit(solution)/shard_map/ppermute | solution.py:15
  18.5 17.2 %copy-start.6 = (bf16[128,1,256]{2,0,1:T(8,128)(2,1)S(1)}, bf16[128,1,256]{2,0,1:T(8,128)(2,1)}, u32[]{:S(2)}) copy-start(bf16[128,1,256]{2,0,1:T(8,128)(2,1)} %param.13) | copy-start | bytes 196612
  24.2 2.1 %copy-start.2 = (f32[2,64,7,128]{3,1,2,0:T(8,128)S(1)}, f32[2,64,7,128]{3,1,2,0:T(8,128)}, u32[]{:S(2)}) copy-start(f32[2,64,7,128]{3,1,2,0:T(8,128)} %get-tuple-element.454) | copy-start | bytes 1376260 | tf_op jit(solution)/shard_map/while
  26.4 0.8 copy-start.3
  32.8 2.1 %copy-start.2 = (f32[2,64,7,128]{3,1,2,0:T(8,128)S(1)}, f32[2,64,7,128]{3,1,2,0:T(8,128)}, u32[]{:S(2)}) copy-start(f32[2,64,7,128]{3,1,2,0:T(8,128)} %get-tuple-element.454) | copy-start | bytes 1376260 | tf_op jit(solution)/shard_map/while
  34.9 0.8 copy-start.3
  35.7 7.0 %copy-start.10 = (f32[2,64,7]{1,2,0:T(8,128)}, f32[2,64,7]{1,2,0:T(8,128)S(1)}, u32[]{:S(2)}) copy-start(f32[2,64,7]{1,2,0:T(8,128)S(1)} %get-tuple-element.100) | copy-start | bytes 10756
  35.7 7.0 %copy-start.12 = (f32[2,64,7]{1,2,0:T(8,128)}, f32[2,64,7]{1,2,0:T(8,128)S(1)}, u32[]{:S(2)}) copy-start(f32[2,64,7]{1,2,0:T(8,128)S(1)} %get-tuple-element.104) | copy-start | bytes 10756
  35.7 3.1 %copy-start.18 = (f32[2,64]{1,0:T(2,128)S(1)}, f32[2,64]{1,0:T(2,128)}, u32[]{:S(2)}) copy-start(f32[2,64]{1,0:T(2,128)} %reduce_sum.73) | copy-start | bytes 1540
  37.0 0.8 copy-start.1
  37.0 1.8 %copy-start.8 = (f32[2,64,7]{1,2,0:T(8,128)}, f32[2,64,7]{1,2,0:T(8,128)S(1)}, u32[]{:S(2)}) copy-start(f32[2,64,7]{1,2,0:T(8,128)S(1)} %get-tuple-element.263) | copy-start | bytes 10756
  46.7 42.5 %copy-start.9 = (f32[2,64,7]{1,2,0:T(8,128)S(1)}, f32[2,64,7]{1,2,0:T(8,128)}, u32[]{:S(2)}) copy-start(f32[2,64,7]{1,2,0:T(8,128)} %copy-done.8) | copy-start | bytes 10756
  46.7 44.1 %copy-start.11 = (f32[2,64,7]{1,2,0:T(8,128)S(1)}, f32[2,64,7]{1,2,0:T(8,128)}, u32[]{:S(2)}) copy-start(f32[2,64,7]{1,2,0:T(8,128)} %copy-done.10) | copy-start | bytes 10756
  46.7 44.1 %copy-start.13 = (f32[2,64,7]{1,2,0:T(8,128)S(1)}, f32[2,64,7]{1,2,0:T(8,128)}, u32[]{:S(2)}) copy-start(f32[2,64,7]{1,2,0:T(8,128)} %copy-done.12) | copy-start | bytes 10756
  46.7 8.3 %copy-start.7 = (bf16[2,64,7,128]{3,1,2,0:T(8,128)(2,1)S(1)}, bf16[2,64,7,128]{3,1,2,0:T(8,128)(2,1)}, u32[]{:S(2)}) copy-start(bf16[2,64,7,128]{3,1,2,0:T(8,128)(2,1)} %get-tuple-element.436) | copy-start | bytes 688132 | tf_op jit(solution)/shard_map/while
  55.7 0.9 copy-start.14
  55.7 0.9 copy-start.16
  56.5 1.0 copy-start.4
  56.6 1.0 copy-start.15
  56.6 1.0 copy-start.17
  57.6 0.8 copy-start.5
  58.4 8.3 %copy-start.7 = (bf16[2,64,7,128]{3,1,2,0:T(8,128)(2,1)S(1)}, bf16[2,64,7,128]{3,1,2,0:T(8,128)(2,1)}, u32[]{:S(2)}) copy-start(bf16[2,64,7,128]{3,1,2,0:T(8,128)(2,1)} %get-tuple-element.436) | copy-start | bytes 688132 | tf_op jit(solution)/shard_map/while
  67.3 0.9 copy-start.14
  67.3 0.9 copy-start.16
  68.2 1.0 copy-start.4
  68.3 1.0 copy-start.15
  68.3 1.0 copy-start.17
  69.3 0.8 copy-start.5
  70.0 20.7 %collective-permute-start.3 = (f32[2,64,7,128]{3,1,2,0:T(8,128)}, f32[2,64,7,128]{3,1,2,0:T(8,128)}, u32[]{:S(2)}, u32[]{:S(2)}) collective-permute-start(f32[2,64,7,128]{3,1,2,0:T(8,128)} %get-tuple-element.103), channel_id=1, source_target_pairs={{4,0},{8,4},{12,8},{16,12},{20,16},{24,20},{28,24},{32,28},{36,32}... | collective-permute-start | bytes 1376264 | tf_op jit(solution)/shard_map/ppermute | solution.py:15
  82.9 7.4 %collective-permute-start.2 = (f32[2,64,7]{1,2,0:T(8,128)}, f32[2,64,7]{1,2,0:T(8,128)S(1)}, u32[]{:S(2)}, u32[]{:S(2)}) collective-permute-start(f32[2,64,7]{1,2,0:T(8,128)} %get-tuple-element.101), channel_id=1, source_target_pairs={{4,0},{8,4},{12,8},{16,12},{20,16},{24,20},{28,24},{32,28},{36,32}... | collective-permute-start | bytes 10760 | tf_op jit(solution)/shard_map/ppermute | solution.py:15
  85.5 5.2 %collective-permute-start.4 = (f32[2,64,7]{1,2,0:T(8,128)}, f32[2,64,7]{1,2,0:T(8,128)S(1)}, u32[]{:S(2)}, u32[]{:S(2)}) collective-permute-start(f32[2,64,7]{1,2,0:T(8,128)} %get-tuple-element.105), channel_id=1, source_target_pairs={{4,0},{8,4},{12,8},{16,12},{20,16},{24,20},{28,24},{32,28},{36,32}... | collective-permute-start | bytes 10760 | tf_op jit(solution)/shard_map/ppermute | solution.py:15
where the time goes:
time: 124 us; the launch traced here: 123 us
  local copies, waits for them, and re-layouts  31.3 us (25%)
  blocking collectives  26.9 us (22%)
  other arithmetic  25.1 us (20%)
  starting transfers between devices  23.1 us (19%)
  matrix products  14.8 us (12%)
    psum x1, blocking collectives, shards(): lax.psum(jnp.dot(attention, o_weight, preferred_element_type=jnp.float32)...  26.9 us
    ppermute x5, starting transfers between devices, from_behind(): return lax.ppermute(block, axis, route)  23.1 us
    gather x4, local copies, waits for them, and re-layouts, one_request(): pages = jnp.take(pool_slots, table_row, axis=0)  8.31 us
    lt x4, other arithmetic, one_request(): visible = positions < length  5.47 us
    dynamic_slice x4, local copies, waits for them, and re-layouts, sweep_all(): return lax.map(one_request, (query_rows, tables, lengths))  5.16 us
    select_n x8, other arithmetic, one_request(): pages = jnp.take(pool_slots, table_row, axis=0)  5.11 us
    dot_general x4, matrix products, pages_partial(): jnp.einsum('tgd,knd->tgkn', query_rows, pages[..., :head_dim], preferred_...  4.09 us
    while x36, local copies, waits for them, and re-layouts  4.06 us
  transfers between devices with their start and end apart: 5, of which 1 were waited for; matrix products, arithmetic and copies ran while one was open for 28% of the time, Pallas kernels for 0%

commit v1 on v0

--- a/solution.py
+++ b/solution.py
@@ -110,7 +110,8 @@
         .reshape(requests * tree_len, group_size * HEAD_SIZE)
     )
     rows_out = attention.shape[0] // lax.axis_size("tp")
-    whole_sum = lax.psum(jnp.dot(attention, o_weight, preferred_element_type=jnp.float32), "tp")
+    test_surface_for = lambda array_here: jnp.sum(lax.all_gather(array_here, "tp"), 0)
+    whole_sum = test_surface_for(jnp.dot(attention, o_weight, preferred_element_type=jnp.float32))
     summed = lax.dynamic_slice_in_dim(whole_sum, lax.axis_index("tp") * rows_out, rows_out, 0)
     projected = summed.astype(jnp.bfloat16)
     node_ids = jnp.arange(tree_len, dtype=jnp.int32)

time: 124 us -> 154 us (1.24)
  the two profiles are of different devices: /device:TPU:8 before, /device:TPU:1 now
where the time goes in v1:
time: 154 us; the launch traced here: 152 us
  waiting for transfers between devices  48.2 us (31%)
  local copies, waits for them, and re-layouts  28.2 us (18%)
  starting transfers between devices  23 us (15%)
  other arithmetic  22.4 us (15%)
  matrix products  16.2 us (11%)
  between operations  14.3 us (9%)
    all_gather x1, waiting for transfers between devices, shards(): lax.all_gather(array_here, 'tp')  46.9 us
    ppermute x5, starting transfers between devices, from_behind(): return lax.ppermute(block, axis, route)  23 us
    gather x4, local copies, waits for them, and re-layouts, one_request(): pages = jnp.take(pool_slots, table_row, axis=0)  8.34 us
    dot_general x4, matrix products, pages_partial(): jnp.einsum('tgd,knd->tgkn', query_rows, pages[..., :head_dim], preferred_...  5.81 us
    select_n x8, other arithmetic, one_request(): pages = jnp.take(pool_slots, table_row, axis=0)  5.13 us
    lt x4, other arithmetic, one_request(): visible = positions < length  4.24 us
    while x24, local copies, waits for them, and re-layouts  4.15 us
    dynamic_slice x4, local copies, waits for them, and re-layouts, sweep_all(): return lax.map(one_request, (query_rows, tables, lengths))  3.88 us
  transfers between devices with their start and end apart: 6, of which 2 were waited for; matrix products, arithmetic and copies ran while one was open for 21% of the time, Pallas kernels for 0%

profile of v1, /device:TPU:1, one launch (start us, length us, event | category | flops | bytes accessed | tf_op | source)
XLA Modules:
  0.0 152.5 jit_solution(13797022251197125763)
XLA Ops:
  7.2 0.9 copy.48
  8.1 1.4 pad_add_fusion
  9.5 4.5 %collective-permute-start = (s32[2,9]{1,0:T(2,128)}, s32[2,9]{1,0:T(2,128)}, u32[]{:S(2)}, u32[]{:S(2)}) collective-permute-start(s32[2,9]{1,0:T(2,128)} %pad_add_fusion), channel_id=1, source_target_pairs={{508,0},{0,4},{4,8},{8,12},{12,16},{16,20},{20,24},{24,28},{28,32}... | collective-permute-start | bytes 224 | tf_op jit(solution)/shard_map/ppermute | solution.py:15
  14.0 1.9 %collective-permute-start.1 = (bf16[128,896]{1,0:T(8,128)(2,1)}, bf16[128,896]{1,0:T(8,128)(2,1)}, u32[]{:S(2)}, u32[]{:S(2)}) collective-permute-start(bf16[128,896]{1,0:T(8,128)(2,1)} %param.12), channel_id=1, source_target_pairs={{508,0},{0,4},{4,8},{8,12},{12,16},{16,20},{20,24},{24,28},{28,32}... | collective-permute-start | bytes 688136 | tf_op jit(solution)/shard_map/ppermute | solution.py:15
  15.9 1.2 reshape.134
  17.7 1.0 convolution_minimum_fusion.5
  19.5 0.8 broadcast_compare_fusion
  20.3 0.8 copy.52
  21.9 0.8 broadcast.143.clone.1
  22.7 17.6 %while.30 = (s32[]{:T(128)}, f32[2,64,7]{1,2,0:T(8,128)S(1)}, f32[2,64,7]{1,2,0:T(8,128)S(1)}, f32[2,64,7,128]{3,1,2,0:T(8,128)}, s32[2]{0:T(128)}, /*index=5*/b...) while((s32[]{:T(128)}, f32[2,64,7]{1,2,0:T(8,128)S(1)}, ...), condition=%wide.region_6.7_spmd.clone, body=%wide.region_0.6_spmd.clone.sunk | while | flops 59991572 | bytes 6568945 | solution.py:82
  23.4 1.7 %gather_fusion = bf16[2,128,256]{2,1,0:T(8,128)(2,1)S(1)} fusion(bf16[12,128,256]{2,1,0:T(8,128)(2,1)} %get-tuple-element.468, s32[1024]{0:T(1024)S(1)} %pad_clamp_fusion.4), kind=kCustom, calls=%fused_computation.clone.clone.1 | custom fusion | bytes 262152 | tf_op jit(solution)/shard_map/while/body/eval_jaxpr/jit(_take)/gather | solution.py:78
  26.0 1.3 dynamic_slice.66
  27.3 1.4 add_compare_fusion.4
  28.7 1.3 fusion.68
  30.7 0.8 copy-done.2
  32.2 1.7 %gather_fusion = bf16[2,128,256]{2,1,0:T(8,128)(2,1)S(1)} fusion(bf16[12,128,256]{2,1,0:T(8,128)(2,1)} %get-tuple-element.468, s32[1024]{0:T(1024)S(1)} %pad_clamp_fusion.4), kind=kCustom, calls=%fused_computation.clone.clone.1 | custom fusion | bytes 262152 | tf_op jit(solution)/shard_map/while/body/eval_jaxpr/jit(_take)/gather | solution.py:78
  34.7 1.3 dynamic_slice.66
  36.1 1.4 add_compare_fusion.4
  37.5 1.3 fusion.68
  39.5 0.8 copy-done.2
  40.3 2.6 %fusion.43 = (f32[2,64,7]{1,2,0:T(8,128)}, f32[2,64,7,64]{1,3,2,0:T(8,128)}) fusion(bf16[2,64,7,128]{3,1,2,0:T(8,128)(2,1)} %get-tuple-element.476, bf16[2,64,256]{2,1,0:T(8,128)(2,1)S(1)} %bitcast.158, pred[2,64,64]{1,2,0:T(8,128)(4,1)S(1)} %copy.52), kind=kOutput, calls=%fused_computation.107 | convolution fusion | flops 14851200 | bytes 511488 | tf_op jit(solution)/shard_map/vmap(tgd,nd->tgn)/dot_general | solution.py:29
  43.5 1.3 slice.29
  44.8 1.3 slice_reduce_fusion
  46.1 1.2 reshape.135
  48.1 0.8 broadcast.143.clone
  48.9 21.1 %while.31 = (s32[]{:T(128)}, f32[2,64,7]{1,2,0:T(8,128)S(1)}, f32[2,64,7]{1,2,0:T(8,128)S(1)}, f32[2,64,7,128]{3,1,2,0:T(8,128)}, s32[2]{0:T(128)}, /*index=5*/b...) while((s32[]{:T(128)}, f32[2,64,7]{1,2,0:T(8,128)S(1)}, ...), condition=%wide.region_13.14_spmd.clone, body=%wide.region_7.13_spmd.clone.sunk | while | flops 180089152 | bytes 10707729 | solution.py:82
  49.7 2.5 %gather_fusion.1 = bf16[6,128,256]{2,1,0:T(8,128)(2,1)} fusion(bf16[12,128,256]{2,1,0:T(8,128)(2,1)} %get-tuple-element.438, s32[1024]{0:T(1024)S(1)} %pad_clamp_fusion.5), kind=kCustom, calls=%fused_computation.1.clone.clone.1 | custom fusion | bytes 786456 | tf_op jit(solution)/shard_map/while/body/eval_jaxpr/jit(_take)/gather | solution.py:78
  52.8 1.1 broadcast_select_fusion.5
  55.3 1.6 %fusion.72 = (f32[64,7,6]{0,2,1:T(8,128)S(1)}, f32[64,7]{0,1:T(8,128)S(1)}, f32[64,7,6,128]{3,0,2,1:T(8,128)S(1)}) fusion(bf16[6,128,256]{2,1,0:T(8,128)(2,1)S(1)} %broadcast_select_fusion.5, bf16[2,64,7,128]{3,1,2,0:T(8,128)(2,1)} %get-tuple-element.436, s32[]{:T(128)} %get-tuple-element.421, pred[6,128]{1,0:T(8,128)(4,1)S(1)} %add_compare_fusion.5), kind=kOutput, calls=%fused_computation.106.clone.1 | convolution fusion | flops 89453504 | bytes 1701632 | tf_op jit(solution)/shard_map/while/body/eval_jaxpr/tgd,knd->tgkn/dot_general | solution.py:51
  56.9 0.8 convert_reduce_fusion.6
  58.7 0.8 copy-done.5
  60.2 2.5 %gather_fusion.1 = bf16[6,128,256]{2,1,0:T(8,128)(2,1)} fusion(bf16[12,128,256]{2,1,0:T(8,128)(2,1)} %get-tuple-element.438, s32[1024]{0:T(1024)S(1)} %pad_clamp_fusion.5), kind=kCustom, calls=%fused_computation.1.clone.clone.1 | custom fusion | bytes 786456 | tf_op jit(solution)/shard_map/while/body/eval_jaxpr/jit(_take)/gather | solution.py:78
  63.4 1.1 broadcast_select_fusion.5
  65.8 1.6 %fusion.72 = (f32[64,7,6]{0,2,1:T(8,128)S(1)}, f32[64,7]{0,1:T(8,128)S(1)}, f32[64,7,6,128]{3,0,2,1:T(8,128)S(1)}) fusion(bf16[6,128,256]{2,1,0:T(8,128)(2,1)S(1)} %broadcast_select_fusion.5, bf16[2,64,7,128]{3,1,2,0:T(8,128)(2,1)} %get-tuple-element.436, s32[]{:T(128)} %get-tuple-element.421, pred[6,128]{1,0:T(8,128)(4,1)S(1)} %add_compare_fusion.5), kind=kOutput, calls=%fused_computation.106.clone.1 | convolution fusion | flops 89453504 | bytes 1701632 | tf_op jit(solution)/shard_map/while/body/eval_jaxpr/tgd,knd->tgkn/dot_general | solution.py:51
  67.4 0.8 convert_reduce_fusion.6
  69.3 0.8 copy-done.5
  70.0 6.3 %collective-permute-start.3 = (f32[2,64,7,128]{3,1,2,0:T(8,128)}, f32[2,64,7,128]{3,1,2,0:T(8,128)S(1)}, u32[]{:S(2)}, u32[]{:S(2)}) collective-permute-start(f32[2,64,7,128]{3,1,2,0:T(8,128)} %get-tuple-element.103), channel_id=1, source_target_pairs={{4,0},{8,4},{12,8},{16,12},{20,16},{24,20},{28,24},{32,28},{36,32}... | collective-permute-start | bytes 1376264 | tf_op jit(solution)/shard_map/ppermute | solution.py:15
  76.3 1.3 fusion.26
  77.6 7.7 %collective-permute-start.2 = (f32[2,64,7]{1,2,0:T(8,128)S(1)}, f32[2,64,7]{1,2,0:T(8,128)S(1)}, u32[]{:S(2)}, u32[]{:S(2)}) collective-permute-start(f32[2,64,7]{1,2,0:T(8,128)S(1)} %get-tuple-element.101), channel_id=1, source_target_pairs={{4,0},{8,4},{12,8},{16,12},{20,16},{24,20},{28,24},{32,28},{36,32}... | collective-permute-start | bytes 10760 | tf_op jit(solution)/shard_map/ppermute | solution.py:15
  85.4 2.5 %collective-permute-start.4 = (f32[2,64,7]{1,2,0:T(8,128)S(1)}, f32[2,64,7]{1,2,0:T(8,128)S(1)}, u32[]{:S(2)}, u32[]{:S(2)}) collective-permute-start(f32[2,64,7]{1,2,0:T(8,128)S(1)} %get-tuple-element.105), channel_id=1, source_target_pairs={{4,0},{8,4},{12,8},{16,12},{20,16},{24,20},{28,24},{32,28},{36,32}... | collective-permute-start | bytes 10760 | tf_op jit(solution)/shard_map/ppermute | solution.py:15
  87.9 1.1 convert_reduce_fusion.2
  89.1 1.3 collective-permute-done.4
  90.4 0.8 divide_convert_fusion
  91.3 1.6 %fusion.21 = f32[128,1792]{1,0:T(8,128)} fusion(bf16[896,1792]{1,0:T(8,128)(2,1)S(1)} %copy-done, bf16[16,8,7,128]{3,2,1,0:T(8,128)(2,1)S(1)} %bitcast.157), kind=kOutput, calls=%fused_computation.68 | convolution fusion | flops 411041792 | bytes 4358144 | tf_op jit(solution)/shard_map/dot_general | solution.py:114
  93.3 0.8 convolution_convert_fusion
  94.1 46.9 %all-gather.3.cloned.1.call-done = f32[512,1792]{1,0:T(8,128)} async-done(((f32[128,1792]{1,0:T(8,128)}), f32[512,1792]{1,0:T(8,128)}) %all-gather.3.cloned.1.call-update) | async-done | bytes 3670032 | tf_op jit(solution)/shard_map/all_gather | solution.py:113
  140.9 3.2 %reduce_sum.82 = bf16[128,1792]{1,0:T(8,128)(2,1)} reduce(f32[4,128,1792]{2,1,0:T(8,128)} %bitcast.156, f32[]{:T(128)} %constant.92.clone.1), dimensions={0}, to_apply=%region_16.17 | reduce | flops 688128 | bytes 4128772 | tf_op jit(solution)/shard_map/reduce_sum | solution.py:113
  144.1 1.6 %dynamic-slice_convert_fusion = bf16[32,1792]{1,0:T(8,128)(2,1)} fusion(bf16[128,1792]{1,0:T(8,128)(2,1)} %reduce_sum.82, s32[]{:T(128)S(6)} %select_n.66), kind=kLoop, calls=%fused_computation.71 | loop fusion | bytes 229380 | tf_op jit(solution)/shard_map/convert_element_type | solution.py:116
  (105 shorter events, 15.7 us)
Async XLA Ops:
  7.2 84.2 %copy-start = (bf16[896,1792]{1,0:T(8,128)(2,1)S(1)}, bf16[896,1792]{1,0:T(8,128)(2,1)}, u32[]{:S(2)}) copy-start(bf16[896,1792]{1,0:T(8,128)(2,1)} %param.19) | copy-start | bytes 9633796
  7.2 133.7 %all-gather.3.cloned.1.call-start = ((), (), s32[]{:S(2)}) async-start(), calls=%async_computation | async-start | bytes 4587520 | tf_op jit(solution)/shard_map/all_gather | solution.py:113
  9.5 34.0 %collective-permute-start = (s32[2,9]{1,0:T(2,128)}, s32[2,9]{1,0:T(2,128)}, u32[]{:S(2)}, u32[]{:S(2)}) collective-permute-start(s32[2,9]{1,0:T(2,128)} %pad_add_fusion), channel_id=1, source_target_pairs={{508,0},{0,4},{4,8},{8,12},{12,16},{16,20},{20,24},{24,28},{28,32}... | collective-permute-start | bytes 224 | tf_op jit(solution)/shard_map/ppermute | solution.py:15
  14.0 32.2 %collective-permute-start.1 = (bf16[128,896]{1,0:T(8,128)(2,1)}, bf16[128,896]{1,0:T(8,128)(2,1)}, u32[]{:S(2)}, u32[]{:S(2)}) collective-permute-start(bf16[128,896]{1,0:T(8,128)(2,1)} %param.12), channel_id=1, source_target_pairs={{508,0},{0,4},{4,8},{8,12},{12,16},{16,20},{20,24},{24,28},{28,32}... | collective-permute-start | bytes 688136 | tf_op jit(solution)/shard_map/ppermute | solution.py:15
  22.7 17.6 %copy-start.6 = (bf16[128,1,256]{2,0,1:T(8,128)(2,1)S(1)}, bf16[128,1,256]{2,0,1:T(8,128)(2,1)}, u32[]{:S(2)}) copy-start(bf16[128,1,256]{2,0,1:T(8,128)(2,1)} %param.13) | copy-start | bytes 196612
  25.1 5.6 %copy-start.1 = (f32[2,64,7,128]{3,1,2,0:T(8,128)S(1)}, f32[2,64,7,128]{3,1,2,0:T(8,128)}, u32[]{:S(2)}) copy-start(f32[2,64,7,128]{3,1,2,0:T(8,128)} %get-tuple-element.454) | copy-start | bytes 1376260 | tf_op jit(solution)/shard_map/while
  30.7 0.8 copy-start.2
  33.9 5.6 %copy-start.1 = (f32[2,64,7,128]{3,1,2,0:T(8,128)S(1)}, f32[2,64,7,128]{3,1,2,0:T(8,128)}, u32[]{:S(2)}) copy-start(f32[2,64,7,128]{3,1,2,0:T(8,128)} %get-tuple-element.454) | copy-start | bytes 1376260 | tf_op jit(solution)/shard_map/while
  39.5 0.8 copy-start.2
  40.3 5.9 %copy-start.9 = (f32[2,64,7]{1,2,0:T(8,128)}, f32[2,64,7]{1,2,0:T(8,128)S(1)}, u32[]{:S(2)}) copy-start(f32[2,64,7]{1,2,0:T(8,128)S(1)} %get-tuple-element.100) | copy-start | bytes 10756
  40.3 5.9 %copy-start.11 = (f32[2,64,7]{1,2,0:T(8,128)}, f32[2,64,7]{1,2,0:T(8,128)S(1)}, u32[]{:S(2)}) copy-start(f32[2,64,7]{1,2,0:T(8,128)S(1)} %get-tuple-element.104) | copy-start | bytes 10756
  48.9 27.4 %copy-start.7 = (bf16[128,1,256]{2,0,1:T(8,128)(2,1)S(1)}, bf16[128,1,256]{2,0,1:T(8,128)(2,1)}, u32[]{:S(2)}) copy-start(bf16[128,1,256]{2,0,1:T(8,128)(2,1)} %param.13) | copy-start | bytes 196612
  48.9 27.4 %copy-start.8 = (f32[2,64,7]{1,2,0:T(8,128)S(1)}, f32[2,64,7]{1,2,0:T(8,128)}, u32[]{:S(2)}) copy-start(f32[2,64,7]{1,2,0:T(8,128)} %get-tuple-element.263) | copy-start | bytes 10756
  48.9 5.0 %copy-start.15 = (s32[2]{0:T(128)S(1)}, s32[2]{0:T(128)}, u32[]{:S(2)}) copy-start(s32[2]{0:T(128)} %get-tuple-element.435) | copy-start | bytes 28 | tf_op jit(solution)/shard_map/while
  49.0 5.6 %copy-start.13 = (s32[6]{0:T(128)S(1)}, s32[6]{0:T(128)}, u32[]{:S(2)}) copy-start(s32[6]{0:T(128)} %get-tuple-element.439) | copy-start | bytes 76 | tf_op jit(solution)/shard_map/while
  57.7 1.0 copy-start.4
  58.7 0.8 copy-start.5
  59.5 5.0 %copy-start.15 = (s32[2]{0:T(128)S(1)}, s32[2]{0:T(128)}, u32[]{:S(2)}) copy-start(s32[2]{0:T(128)} %get-tuple-element.435) | copy-start | bytes 28 | tf_op jit(solution)/shard_map/while
  59.5 5.6 %copy-start.13 = (s32[6]{0:T(128)S(1)}, s32[6]{0:T(128)}, u32[]{:S(2)}) copy-start(s32[6]{0:T(128)} %get-tuple-element.439) | copy-start | bytes 76 | tf_op jit(solution)/shard_map/while
  68.2 1.0 copy-start.4
  69.2 0.8 copy-start.5
  70.0 20.3 %copy-start.10 = (f32[2,64,7]{1,2,0:T(8,128)S(1)}, f32[2,64,7]{1,2,0:T(8,128)}, u32[]{:S(2)}) copy-start(f32[2,64,7]{1,2,0:T(8,128)} %copy-done.9) | copy-start | bytes 10756
  70.0 20.3 %copy-start.12 = (f32[2,64,7]{1,2,0:T(8,128)S(1)}, f32[2,64,7]{1,2,0:T(8,128)}, u32[]{:S(2)}) copy-start(f32[2,64,7]{1,2,0:T(8,128)} %copy-done.11) | copy-start | bytes 10756
  70.0 20.3 %copy-start.3 = (f32[2,64,7,128]{3,1,2,0:T(8,128)S(1)}, f32[2,64,7,128]{3,1,2,0:T(8,128)}, u32[]{:S(2)}) copy-start(f32[2,64,7,128]{3,1,2,0:T(8,128)} %get-tuple-element.102) | copy-start | bytes 1376260
  70.0 20.3 %collective-permute-start.3 = (f32[2,64,7,128]{3,1,2,0:T(8,128)}, f32[2,64,7,128]{3,1,2,0:T(8,128)S(1)}, u32[]{:S(2)}, u32[]{:S(2)}) collective-permute-start(f32[2,64,7,128]{3,1,2,0:T(8,128)} %get-tuple-element.103), channel_id=1, source_target_pairs={{4,0},{8,4},{12,8},{16,12},{20,16},{24,20},{28,24},{32,28},{36,32}... | collective-permute-start | bytes 1376264 | tf_op jit(solution)/shard_map/ppermute | solution.py:15
  77.6 11.4 %collective-permute-start.2 = (f32[2,64,7]{1,2,0:T(8,128)S(1)}, f32[2,64,7]{1,2,0:T(8,128)S(1)}, u32[]{:S(2)}, u32[]{:S(2)}) collective-permute-start(f32[2,64,7]{1,2,0:T(8,128)S(1)} %get-tuple-element.101), channel_id=1, source_target_pairs={{4,0},{8,4},{12,8},{16,12},{20,16},{24,20},{28,24},{32,28},{36,32}... | collective-permute-start | bytes 10760 | tf_op jit(solution)/shard_map/ppermute | solution.py:15
  85.4 5.0 %collective-permute-start.4 = (f32[2,64,7]{1,2,0:T(8,128)S(1)}, f32[2,64,7]{1,2,0:T(8,128)S(1)}, u32[]{:S(2)}, u32[]{:S(2)}) collective-permute-start(f32[2,64,7]{1,2,0:T(8,128)S(1)} %get-tuple-element.105), channel_id=1, source_target_pairs={{4,0},{8,4},{12,8},{16,12},{20,16},{24,20},{28,24},{32,28},{36,32}... | collective-permute-start | bytes 10760 | tf_op jit(solution)/shard_map/ppermute | solution.py:15
  91.3 1.7 %copy-start.14 = (s32[2]{0:T(128)S(1)}, s32[2]{0:T(128)}, u32[]{:S(2)}) copy-start(s32[2]{0:T(128)} %param.18) | copy-start | bytes 28
Sparse Core Ops, SparseCore 0:
  93.1 47.8 all-gather.2
